TPU v7x, 32 devices: a whole 2x2x4 slice. The times are simulated.
32 devices in a mesh: dp: 4 (over z), fsdp: 2 (over x), rows: 4 (over y, core).
Axes of the slice: x: 2, y: 2, z: 4, core: 2. Of those that a mesh axis runs over, the one named last changes fastest.
Arguments:
- feature_maps: bfloat16 [8, 16, 32, 1536], P(('dp', 'fsdp'), 'rows'), may hold values from -30 to 30
- dw_kernel: float32 [7, 7, 1536], replicated, may hold values from -0.875 to 0.875
- norm_gain: float32 [1536], replicated, may hold values from 0.5 to 1.5
- w_up: bfloat16 [1536, 6144], P(('dp', 'rows'), 'fsdp'), may hold values from -0.15625 to 0.15625
- w_down: bfloat16 [6144, 1536], P('fsdp', ('dp', 'rows')), may hold values from -0.078125 to 0.078125
- layer_scale: float32 [1536], replicated, may hold values from 0.3 to 1.5
- d_out: bfloat16 [8, 16, 32, 1536], P(('dp', 'fsdp'), 'rows'), may hold values from -20 to 20
Outputs:
- result: bfloat16 [8, 16, 32, 1536], P(('dp', 'fsdp'), 'rows')
- grad_x: bfloat16 [8, 16, 32, 1536], P(('dp', 'fsdp'), 'rows')
- grad_up: float32 [1536, 6144], P(('dp', 'rows'), 'fsdp')
- grad_down: float32 [6144, 1536], P('fsdp', ('dp', 'rows'))
- grad_kernel: float32 [7, 7, 1536], replicated
- grad_gain: float32 [1536], replicated
- grad_scale: float32 [1536], replicated
All inputs are finite; a program needn't handle non-finite values.
Results may differ from a plain program's by a relative error of at most 0.0075.
Values may be sent and summed in bfloat16 or wider, within the bound.
No kernel may reach another device: no remote copies, remote signals or barrier semaphores. Data moves between devices by JAX's collectives and lax.ppermute only.
A program may use at most 128 MiB of HBM per device.

v0:
```python
import math
import jax
import jax.numpy as jnp
from jax import lax
from jax.sharding import PartitionSpec as P

KS = 7
norm_eps = 1e-06
inv_root_two = 1.0 / math.sqrt(2.0)
inv_root_two_pi = 1.0 / math.sqrt(2.0 * math.pi)
contract_rows = (((0,), (0,)), ((), ()))
contract_cols = (((1,), (1,)), ((), ()))


def padded_2(x, sides, width):
    for axis, dim in sides:
        devices, length = (lax.axis_size(axis), x.shape[dim])
        up = [(i, (i + 1) % devices) for i in range(devices - 1)]
        down = [(j, i) for i, j in up]
        last = lax.slice_in_dim(x, length - width, length, axis=dim)
        leading = lax.slice_in_dim(x, 0, width, axis=dim)
        before = lax.ppermute(last, axis, up)
        after = lax.ppermute(leading, axis, down)
        x = jnp.concatenate([before, x, after], axis=dim)
    return x


def gelu_exact(values):
    return 0.5 * values * (1.0 + jax.scipy.special.erf(values * inv_root_two))


def gelu_slope(values):
    cdf_part = 0.5 * (1.0 + jax.scipy.special.erf(values * inv_root_two))
    return cdf_part + values * jnp.exp(-0.5 * values * values) * inv_root_two_pi


def small_sums(kernel_part, gain_part, scale_part, width):
    every = ("dp", "fsdp", "rows")
    devices = lax.axis_size(every)
    packed = jnp.concatenate(
        [kernel_part.reshape(KS * KS, width), gain_part[None], scale_part[None]], axis=0
    )
    count = packed.shape[0]
    per = -(-count // devices)
    packed = jnp.pad(packed, ((0, per * devices - count), (0, 0)))
    mine = lax.all_to_all(packed.reshape(devices, per, width), every, 0, 0, tiled=True).sum(0)
    spread = jnp.broadcast_to(mine[None], (devices, per, width))
    total = lax.all_to_all(spread, every, 0, 0, tiled=True).reshape(devices * per, width)
    kernel_sum = total[: KS * KS].reshape(KS, KS, width)
    return (kernel_sum, total[KS * KS], total[KS * KS + 1])


def body(feature_maps, dw_kernel, norm_gain, w_up, w_down, layer_scale, d_out):
    scenes, strip, across, width = feature_maps.shape
    cells = scenes * strip * across
    hid_axes = ("fsdp", "rows")
    dp_size, row_size = (lax.axis_size("dp"), lax.axis_size("rows"))
    block_c, hid_f = w_up.shape
    sub = hid_f // row_size
    pieces = w_up.reshape(block_c, row_size, sub).transpose(1, 0, 2)
    pieces = jnp.broadcast_to(pieces[None], (dp_size, row_size, block_c, sub))
    pieces = pieces.reshape(dp_size * row_size, block_c, sub)
    up_loc = lax.all_to_all(pieces, ("dp", "rows"), 0, 0, tiled=True)
    up_loc = up_loc.reshape(dp_size * row_size * block_c, sub)
    down_loc = lax.all_to_all(w_down, "rows", 0, 1, tiled=True)
    down_loc = lax.all_gather(down_loc, "dp", axis=1, tiled=True)
    cotan = d_out.reshape(cells, width).astype(jnp.float32)
    back = (cotan * layer_scale).astype(jnp.bfloat16)
    rimmed = padded_2(feature_maps, (("rows", 1),), 3)
    padded = jnp.pad(rimmed.astype(jnp.float32), ((0, 0), (0, 0), (3, 3), (0, 0)))
    filtered = jnp.zeros(feature_maps.shape, jnp.float32)
    for row_off in range(KS):
        for col_off in range(KS):
            filtered = (
                filtered
                + padded[:, row_off : row_off + strip, col_off : col_off + across, :]
                * dw_kernel[row_off, col_off]
            )
    flat = filtered.reshape(cells, width)
    average = jnp.mean(flat, axis=-1, keepdims=True)
    center = flat - average
    variance = jnp.mean(center * center, axis=-1, keepdims=True)
    rstd = lax.rsqrt(variance + norm_eps)
    normed = center * rstd
    scaled = (normed * norm_gain).astype(jnp.bfloat16)
    pair = lax.all_gather(jnp.stack([scaled, back]), hid_axes, axis=1, tiled=True)
    gathered, back_all = (pair[0], pair[1])
    hidden = jnp.dot(gathered, up_loc, preferred_element_type=jnp.float32)
    active = gelu_exact(hidden).astype(jnp.bfloat16)
    mlp_terms = jnp.dot(active, down_loc, preferred_element_type=jnp.float32)
    down_part_t = lax.dot_general(
        back_all, active, contract_rows, preferred_element_type=jnp.float32
    )
    slope_in = lax.dot_general(
        back_all, down_loc, contract_cols, preferred_element_type=jnp.float32
    )
    hidden_grad = (slope_in * gelu_slope(hidden)).astype(jnp.bfloat16)
    up_part = lax.dot_general(
        gathered, hidden_grad, contract_rows, preferred_element_type=jnp.float32
    )
    norm_terms = lax.dot_general(
        hidden_grad, up_loc, contract_cols, preferred_element_type=jnp.float32
    )
    sums = lax.psum_scatter(
        jnp.stack([mlp_terms, norm_terms]).astype(jnp.bfloat16),
        hid_axes,
        scatter_dimension=1,
        tiled=True,
    ).astype(jnp.float32)
    branch, norm_grad = (sums[0], sums[1])
    resid = feature_maps.reshape(cells, width).astype(jnp.float32)
    result = (resid + layer_scale * branch).astype(jnp.bfloat16).reshape(feature_maps.shape)
    scale_part = jnp.sum(cotan * branch, axis=0)
    down_blocks = down_part_t.astype(jnp.bfloat16).reshape(dp_size, -1, sub)
    down_sum = lax.all_to_all(down_blocks, "dp", 0, 0, tiled=True).astype(jnp.float32).sum(0)
    up_sum = lax.psum_scatter(up_part.astype(jnp.bfloat16), "dp", scatter_dimension=0, tiled=True)
    grad_sums = jnp.stack([up_sum, down_sum.astype(jnp.bfloat16)])
    gain_part = jnp.sum(norm_grad * normed, axis=0)
    scaled_grad = norm_grad * norm_gain
    conv_grad = rstd * (
        scaled_grad
        - jnp.mean(scaled_grad, axis=-1, keepdims=True)
        - normed * jnp.mean(scaled_grad * normed, axis=-1, keepdims=True)
    )
    conv_grad = conv_grad.reshape(feature_maps.shape)
    grad_rim = padded_2(conv_grad.astype(jnp.bfloat16), (("rows", 1),), 3).astype(conv_grad.dtype)
    grad_pad = jnp.pad(grad_rim, ((0, 0), (0, 0), (3, 3), (0, 0)))
    kernel_rows = []
    back_conv = jnp.zeros(feature_maps.shape, jnp.float32)
    for row_off in range(KS):
        for col_off in range(KS):
            window = padded[:, row_off : row_off + strip, col_off : col_off + across, :]
            kernel_rows.append(jnp.sum(window * conv_grad, axis=(0, 1, 2)))
            back_conv = (
                back_conv
                + grad_pad[
                    :, 6 - row_off : 6 - row_off + strip, 6 - col_off : 6 - col_off + across, :
                ]
                * dw_kernel[row_off, col_off]
            )
    kernel_part = jnp.stack(kernel_rows).reshape(KS, KS, width)
    grad_x = (d_out.astype(jnp.float32) + back_conv).astype(jnp.bfloat16)
    grad_kernel, grad_gain, grad_scale = small_sums(kernel_part, gain_part, scale_part, width)
    grad_sums, grad_x, grad_kernel, grad_gain, grad_scale = lax.optimization_barrier(
        (grad_sums, grad_x, grad_kernel, grad_gain, grad_scale)
    )
    grad_sums = lax.all_to_all(grad_sums, "rows", 1, 2, tiled=True).astype(jnp.float32)
    grad_up, grad_down = (grad_sums[0], grad_sums[1].T)
    return (result, grad_x, grad_up, grad_down, grad_kernel, grad_gain, grad_scale)


def solution(mesh):
    return jax.shard_map(
        body,
        mesh=mesh,
        in_specs=(
            P(("dp", "fsdp"), "rows", None, None),
            P(),
            P(),
            P(("dp", "rows"), "fsdp"),
            P("fsdp", ("dp", "rows")),
            P(),
            P(("dp", "fsdp"), "rows", None, None),
        ),
        out_specs=(
            P(("dp", "fsdp"), "rows", None, None),
            P(("dp", "fsdp"), "rows", None, None),
            P(("dp", "rows"), "fsdp"),
            P("fsdp", ("dp", "rows")),
            P(),
            P(),
            P(),
        ),
        check_vma=False,
    )
```

profile of v0, /device:TPU:0, one launch (start us, length us, event | category | flops | bytes accessed | tf_op | source)
XLA Modules:
  0.0 350.1 jit_solution(6042365886521894993)
XLA Ops:
  15.4 2.5 slice_reduce_fusion.49
  19.2 9.4 %fusion.110 = (f32[4,32]{1,0:T(4,128)S(1)}, f32[1,4,32,1536]{3,2,1,0:T(8,128)S(1)}) fusion(f32[1536]{0:T(1024)S(1)} %get-tuple-element.119, f32[1536]{0:T(1024)S(1)} %get-tuple-element.120, f32[1536]{0:T(1024)S(1)} %get-tuple-element.73, f32[1536]{0:T(1024)S(1)} %get-tuple-element.74, f32[1,10,32,1536]{3,2,1,0:T(8,128)S(1)} %maximum_convert_fusion, ...), kind=kLoop, calls=%fused_computation.332 | loop fusion | flops 19267456 | bytes 8641024 | tf_op jit(solution)/shard_map/reduce_sum | solution.py:80
  31.9 6.1 %all-to-all-start.1 = ((bf16[4,768,96]{1,2,0:T(8,128)(2,1)}), bf16[4,768,96]{1,2,0:T(8,128)(2,1)S(1)}, u32[]{:S(2)}, u32[]{:S(2)}) async-start(bf16[4,768,96]{1,2,0:T(8,128)(2,1)} %bitcast.94), calls=%async_computation.1 | async-start | bytes 1179648 | tf_op jit(solution)/shard_map/all_to_all | solution.py:65
  42.5 7.0 %all-to-all-done.1 = bf16[4,768,96]{1,2,0:T(8,128)(2,1)S(1)} async-done(((bf16[4,768,96]{1,2,0:T(8,128)(2,1)}), bf16[4,768,96]{1,2,0:T(8,128)(2,1)S(1)}, u32[]{:S(2)}, u32[]{:S(2)}) %all-to-all-start.1) | async-done | bytes 589856 | tf_op jit(solution)/shard_map/all_to_all | solution.py:65
  49.5 2.9 broadcast_in_dim.8
  52.4 5.3 %all-to-all-start = ((bf16[16,96,768]{2,1,0:T(8,128)(2,1)}), bf16[16,96,768]{2,1,0:T(8,128)(2,1)}, u32[]{:S(2)}, u32[]{:S(2)}) async-start(bf16[16,96,768]{2,1,0:T(8,128)(2,1)} %bitcast.86), calls=%async_computation | async-start | bytes 4718592 | tf_op jit(solution)/shard_map/all_to_all | solution.py:63
  58.8 44.8 %all-to-all-done = bf16[16,96,768]{2,1,0:T(8,128)(2,1)} async-done(((bf16[16,96,768]{2,1,0:T(8,128)(2,1)}), bf16[16,96,768]{2,1,0:T(8,128)(2,1)}, u32[]{:S(2)}, u32[]{:S(2)}) %all-to-all-start) | async-done | bytes 2359328 | tf_op jit(solution)/shard_map/all_to_all | solution.py:63
  103.6 7.5 %multiply_convert_fusion = (bf16[1024,768]{1,0:T(8,128)(2,1)}, f32[1024,768]{1,0:T(8,128)}) fusion(bf16[1536,768]{1,0:T(8,128)(2,1)} %bitcast.5, bf16[2,1024,1536]{2,1,0:T(8,128)(2,1)} %all-gather.3.cloned.1.call-done), kind=kOutput, calls=%fused_computation.100 | convolution fusion | flops 2419851264 | bytes 10223616 | tf_op jit(solution)/shard_map/dot_general | solution.py:88
  111.1 43.2 %all-gather.5.cloned.1.call-done = bf16[768,1536]{0,1:T(8,128)(2,1)} async-done(((bf16[768,384]{0,1:T(8,128)(2,1)}), bf16[768,1536]{0,1:T(8,128)(2,1)}) %all-gather.5.cloned.1.call-update) | async-done | bytes 2359312 | tf_op jit(solution)/shard_map/all_gather | solution.py:66
  154.3 6.6 %fusion.7 = bf16[1024,768]{1,0:T(8,128)(2,1)S(1)} fusion(f32[1024,768]{1,0:T(8,128)} %get-tuple-element.134, bf16[768,1536]{0,1:T(8,128)(2,1)} %all-gather.5.cloned.1.call-done, bf16[2,1024,1536]{2,1,0:T(8,128)(2,1)} %all-gather.3.cloned.1.call-done), kind=kOutput, calls=%fused_computation.97 | convolution fusion | flops 2423783424 | bytes 10223616 | tf_op jit(solution)/shard_map/dot_general | solution.py:94
  161.0 5.1 %fusion.1 = bf16[1,1024,1536]{2,1,0:T(8,128)(2,1)S(1)} fusion(bf16[1024,768]{1,0:T(8,128)(2,1)S(1)} %fusion.7, bf16[1536,768]{1,0:T(8,128)(2,1)} %bitcast.5), kind=kOutput, calls=%fused_computation.91 | convolution fusion | flops 2417491968 | bytes 7077888 | tf_op jit(solution)/shard_map/dot_general | solution.py:101
  166.1 2.9 fusion
  169.1 3.2 pad_maximum_fusion
  172.8 6.5 %convolution_convert_fusion.3 = bf16[1536,768]{1,0:T(8,128)(2,1)} fusion(bf16[1024,768]{1,0:T(8,128)(2,1)} %copy-done.61, bf16[2,1024,1536]{2,1,0:T(8,128)(2,1)} %all-gather.3.cloned.1.call-done), kind=kOutput, calls=%fused_computation.89 | convolution fusion | flops 2417098752 | bytes 7077888 | tf_op jit(solution)/shard_map/dot_general | solution.py:98
  179.3 7.1 %convolution_convert_fusion.2 = bf16[1536,768]{1,0:T(8,128)(2,1)} fusion(bf16[1024,768]{1,0:T(8,128)(2,1)} %get-tuple-element.133, bf16[2,1024,1536]{2,1,0:T(8,128)(2,1)} %all-gather.3.cloned.1.call-done), kind=kOutput, calls=%fused_computation.88 | convolution fusion | flops 2417098752 | bytes 7077888 | tf_op jit(solution)/shard_map/dot_general | solution.py:91
  186.4 4.5 %all-to-all-start.2 = ((bf16[4,384,768]{2,1,0:T(8,128)(2,1)}), bf16[4,384,768]{2,1,0:T(8,128)(2,1)}, u32[]{:S(2)}, u32[]{:S(2)}) async-start(bf16[4,384,768]{2,1,0:T(8,128)(2,1)} %bitcast.92), calls=%async_computation.4 | async-start | bytes 4718592 | tf_op jit(solution)/shard_map/all_to_all | solution.py:115
  190.9 42.1 %reduce-scatter.3.cloned.1.call-done = bf16[2,128,1536]{2,1,0:T(8,128)(2,1)} async-done(((bf16[2,1024,1536]{2,1,0:T(8,128)(2,1)}), bf16[2,128,1536]{2,1,0:T(8,128)(2,1)}) %reduce-scatter.3.cloned.1.call-update) | async-done | bytes 786448 | tf_op jit(solution)/shard_map/reduce_scatter | solution.py:104
  251.8 4.7 %all-to-all-start.3 = ((f32[32,2,1536]{2,1,0:T(2,128)}), f32[32,2,1536]{2,1,0:T(2,128)}, u32[]{:S(2)}, u32[]{:S(2)}) async-start(f32[32,2,1536]{2,1,0:T(2,128)} %reshape.563), calls=%async_computation.5 | async-start | bytes 786432 | tf_op jit(solution)/shard_map/all_to_all | solution.py:46
  262.5 27.8 %reduce-scatter.5.cloned.1.call-done = bf16[384,768]{1,0:T(8,128)(2,1)} async-done(((bf16[1536,768]{1,0:T(8,128)(2,1)}), bf16[384,768]{1,0:T(8,128)(2,1)}) %reduce-scatter.5.cloned.1.call-update) | async-done | bytes 589840 | tf_op jit(solution)/shard_map/reduce_scatter | solution.py:116
  295.3 4.9 %all-to-all-start.4 = ((f32[32,2,1536]{2,1,0:T(2,128)}), f32[32,2,1536]{2,1,0:T(2,128)S(1)}, u32[]{:S(2)}, u32[]{:S(2)}) async-start(f32[32,2,1536]{2,1,0:T(2,128)} %broadcast_in_dim.11), calls=%async_computation.6 | async-start | bytes 786432 | tf_op jit(solution)/shard_map/all_to_all | solution.py:48
  300.3 8.3 %fusion.97 = bf16[1,4,32,1536]{3,2,1,0:T(8,128)(2,1)} fusion(f32[1,10,32,1536]{3,2,1,0:T(8,128)S(1)} %maximum_convert_fusion.1, f32[1536]{0:T(1024)} %copy-done.16, f32[1536]{0:T(1024)} %copy-done.17, f32[1536]{0:T(1024)} %copy-done.19, f32[1536]{0:T(1024)} %copy-done.20, f32[1536]{0:T(1024)} %copy-done.21, f32[1536]{0:T(1024)} %copy-done.22, ...), kind=kLoop, calls=%fused_computation.195 | loop fusion | flops 19660800 | bytes 8562688 | tf_op jit(solution)/shard_map/convert_element_type | solution.py:142
  308.6 4.8 %all-to-all-done.4 = f32[32,2,1536]{2,1,0:T(2,128)S(1)} async-done(((f32[32,2,1536]{2,1,0:T(2,128)}), f32[32,2,1536]{2,1,0:T(2,128)S(1)}, u32[]{:S(2)}, u32[]{:S(2)}) %all-to-all-start.4) | async-done | bytes 393248 | tf_op jit(solution)/shard_map/all_to_all | solution.py:48
  317.4 3.5 %all-to-all-start.5 = ((bf16[2,384,768]{2,0,1:T(2,128)(2,1)}), bf16[2,384,768]{2,0,1:T(2,128)(2,1)S(1)}, u32[]{:S(2)}, u32[]{:S(2)}) async-start(bf16[2,384,768]{2,0,1:T(2,128)(2,1)} %copy.37), calls=%async_computation.7 | async-start | bytes 2359296 | tf_op jit(solution)/shard_map/all_to_all | solution.py:147
  322.9 13.8 %all-to-all-done.5 = bf16[2,384,768]{2,0,1:T(2,128)(2,1)S(1)} async-done(((bf16[2,384,768]{2,0,1:T(2,128)(2,1)}), bf16[2,384,768]{2,0,1:T(2,128)(2,1)S(1)}, u32[]{:S(2)}, u32[]{:S(2)}) %all-to-all-start.5) | async-done | bytes 1179680 | tf_op jit(solution)/shard_map/all_to_all | solution.py:147
  (239 shorter events, 59.9 us)
Async XLA Ops:
  7.2 96.4 %all-gather.3.cloned.1.call-start = ((), (), s32[]{:S(2)}) async-start(), calls=%async_computation.8 | async-start | bytes 7077888 | tf_op jit(solution)/shard_map/all_gather | solution.py:86
  8.3 9.7 %collective-permute-start = (bf16[1,3,32,1536]{3,2,1,0:T(8,128)(2,1)S(1)}, bf16[1,3,32,1536]{3,2,1,0:T(8,128)(2,1)S(1)}, u32[]{:S(2)}, u32[]{:S(2)}) collective-permute-start(bf16[1,3,32,1536]{3,2,1,0:T(8,128)(2,1)S(1)} %get-tuple-element.131), channel_id=1, source_target_pairs={{0,1},{1,2},{2,3},{4,5},{5,6},{6,7},{8,9},{9,10},{10,11},{12,13},{... | collective-permute-start | bytes 884744 | tf_op jit(solution)/shard_map/ppermute | solution.py:22
  10.7 7.3 %collective-permute-start.1 = (bf16[1,3,32,1536]{3,2,1,0:T(8,128)(2,1)S(1)}, bf16[1,3,32,1536]{3,2,1,0:T(8,128)(2,1)S(1)}, u32[]{:S(2)}, u32[]{:S(2)}) collective-permute-start(bf16[1,3,32,1536]{3,2,1,0:T(8,128)(2,1)S(1)} %get-tuple-element.132), channel_id=1, source_target_pairs={{1,0},{2,1},{3,2},{5,4},{6,5},{7,6},{9,8},{10,9},{11,10},{13,12},{... | collective-permute-start | bytes 884744 | tf_op jit(solution)/shard_map/ppermute | solution.py:23
  13.4 15.3 %copy-start.7 = (f32[1536]{0:T(1024)}, f32[1536]{0:T(1024)S(1)}, u32[]{:S(2)}) copy-start(f32[1536]{0:T(1024)S(1)} %get-tuple-element.111) | copy-start | bytes 18436
  13.4 15.3 %copy-start.9 = (f32[1536]{0:T(1024)}, f32[1536]{0:T(1024)S(1)}, u32[]{:S(2)}) copy-start(f32[1536]{0:T(1024)S(1)} %get-tuple-element.112) | copy-start | bytes 18436
  13.4 15.3 %copy-start.10 = (f32[1536]{0:T(1024)}, f32[1536]{0:T(1024)S(1)}, u32[]{:S(2)}) copy-start(f32[1536]{0:T(1024)S(1)} %get-tuple-element.113) | copy-start | bytes 18436
  13.4 15.3 %copy-start.11 = (f32[1536]{0:T(1024)}, f32[1536]{0:T(1024)S(1)}, u32[]{:S(2)}) copy-start(f32[1536]{0:T(1024)S(1)} %get-tuple-element.114) | copy-start | bytes 18436
  13.4 15.3 %copy-start.12 = (f32[1536]{0:T(1024)}, f32[1536]{0:T(1024)S(1)}, u32[]{:S(2)}) copy-start(f32[1536]{0:T(1024)S(1)} %get-tuple-element.115) | copy-start | bytes 18436
  13.4 15.3 %copy-start.13 = (f32[1536]{0:T(1024)}, f32[1536]{0:T(1024)S(1)}, u32[]{:S(2)}) copy-start(f32[1536]{0:T(1024)S(1)} %get-tuple-element.116) | copy-start | bytes 18436
  13.4 15.3 %copy-start.14 = (f32[1536]{0:T(1024)}, f32[1536]{0:T(1024)S(1)}, u32[]{:S(2)}) copy-start(f32[1536]{0:T(1024)S(1)} %get-tuple-element.117) | copy-start | bytes 18436
  13.4 15.3 %copy-start.15 = (f32[1536]{0:T(1024)}, f32[1536]{0:T(1024)S(1)}, u32[]{:S(2)}) copy-start(f32[1536]{0:T(1024)S(1)} %get-tuple-element.118) | copy-start | bytes 18436
  13.5 15.3 %copy-start.16 = (f32[1536]{0:T(1024)}, f32[1536]{0:T(1024)S(1)}, u32[]{:S(2)}) copy-start(f32[1536]{0:T(1024)S(1)} %get-tuple-element.119) | copy-start | bytes 18436
  13.5 15.3 %copy-start.17 = (f32[1536]{0:T(1024)}, f32[1536]{0:T(1024)S(1)}, u32[]{:S(2)}) copy-start(f32[1536]{0:T(1024)S(1)} %get-tuple-element.120) | copy-start | bytes 18436
  31.9 17.6 %all-to-all-start.1 = ((bf16[4,768,96]{1,2,0:T(8,128)(2,1)}), bf16[4,768,96]{1,2,0:T(8,128)(2,1)S(1)}, u32[]{:S(2)}, u32[]{:S(2)}) async-start(bf16[4,768,96]{1,2,0:T(8,128)(2,1)} %bitcast.94), calls=%async_computation.1 | async-start | bytes 1179648 | tf_op jit(solution)/shard_map/all_to_all | solution.py:65
  52.4 51.2 %all-to-all-start = ((bf16[16,96,768]{2,1,0:T(8,128)(2,1)}), bf16[16,96,768]{2,1,0:T(8,128)(2,1)}, u32[]{:S(2)}, u32[]{:S(2)}) async-start(bf16[16,96,768]{2,1,0:T(8,128)(2,1)} %bitcast.86), calls=%async_computation | async-start | bytes 4718592 | tf_op jit(solution)/shard_map/all_to_all | solution.py:63
  57.7 96.6 %all-gather.5.cloned.1.call-start = ((), (), s32[]{:S(2)}) async-start(), calls=%async_computation.9 | async-start | bytes 2949120 | tf_op jit(solution)/shard_map/all_gather | solution.py:66
  58.5 174.5 %reduce-scatter.3.cloned.1.call-start = ((), (), s32[]{:S(2)}) async-start(), calls=%async_computation.10 | async-start | bytes 7077888 | tf_op jit(solution)/shard_map/reduce_scatter | solution.py:104
  172.3 118.0 %reduce-scatter.5.cloned.1.call-start = ((), (), s32[]{:S(2)}) async-start(), calls=%async_computation.11 | async-start | bytes 2949120 | tf_op jit(solution)/shard_map/reduce_scatter | solution.py:116
  186.4 65.4 %all-to-all-start.2 = ((bf16[4,384,768]{2,1,0:T(8,128)(2,1)}), bf16[4,384,768]{2,1,0:T(8,128)(2,1)}, u32[]{:S(2)}, u32[]{:S(2)}) async-start(bf16[4,384,768]{2,1,0:T(8,128)(2,1)} %bitcast.92), calls=%async_computation.4 | async-start | bytes 4718592 | tf_op jit(solution)/shard_map/all_to_all | solution.py:115
  251.8 41.5 %all-to-all-start.3 = ((f32[32,2,1536]{2,1,0:T(2,128)}), f32[32,2,1536]{2,1,0:T(2,128)}, u32[]{:S(2)}, u32[]{:S(2)}) async-start(f32[32,2,1536]{2,1,0:T(2,128)} %reshape.563), calls=%async_computation.5 | async-start | bytes 786432 | tf_op jit(solution)/shard_map/all_to_all | solution.py:46
  256.6 34.9 %collective-permute-start.2 = (bf16[1,3,32,1536]{3,2,1,0:T(8,128)(2,1)S(1)}, bf16[1,3,32,1536]{3,2,1,0:T(8,128)(2,1)S(1)}, u32[]{:S(2)}, u32[]{:S(2)}) collective-permute-start(bf16[1,3,32,1536]{3,2,1,0:T(8,128)(2,1)S(1)} %get-tuple-element.129), channel_id=1, source_target_pairs={{0,1},{1,2},{2,3},{4,5},{5,6},{6,7},{8,9},{9,10},{10,11},{12,13},{... | collective-permute-start | bytes 884744 | tf_op jit(solution)/shard_map/ppermute | solution.py:22
  258.7 33.5 %collective-permute-start.3 = (bf16[1,3,32,1536]{3,2,1,0:T(8,128)(2,1)S(1)}, bf16[1,3,32,1536]{3,2,1,0:T(8,128)(2,1)}, u32[]{:S(2)}, u32[]{:S(2)}) collective-permute-start(bf16[1,3,32,1536]{3,2,1,0:T(8,128)(2,1)S(1)} %get-tuple-element.130), channel_id=1, source_target_pairs={{1,0},{2,1},{3,2},{5,4},{6,5},{7,6},{9,8},{10,9},{11,10},{13,12},{... | collective-permute-start | bytes 884744 | tf_op jit(solution)/shard_map/ppermute | solution.py:23
  295.3 18.1 %all-to-all-start.4 = ((f32[32,2,1536]{2,1,0:T(2,128)}), f32[32,2,1536]{2,1,0:T(2,128)S(1)}, u32[]{:S(2)}, u32[]{:S(2)}) async-start(f32[32,2,1536]{2,1,0:T(2,128)} %broadcast_in_dim.11), calls=%async_computation.6 | async-start | bytes 786432 | tf_op jit(solution)/shard_map/all_to_all | solution.py:48
  317.4 19.4 %all-to-all-start.5 = ((bf16[2,384,768]{2,0,1:T(2,128)(2,1)}), bf16[2,384,768]{2,0,1:T(2,128)(2,1)S(1)}, u32[]{:S(2)}, u32[]{:S(2)}) async-start(bf16[2,384,768]{2,0,1:T(2,128)(2,1)} %copy.37), calls=%async_computation.7 | async-start | bytes 2359296 | tf_op jit(solution)/shard_map/all_to_all | solution.py:147
  (52 other events, 469.7 us)
Sparse Core Ops, SparseCore 0:
  30.9 67.5 all-gather.2
  100.6 53.6 all-gather.4
  172.4 60.5 reduce-scatter.2
  235.3 54.9 reduce-scatter.4
where the time goes:
time: 357 us; the launch traced here: 350 us
  waiting for transfers between devices  184 us (52%)
  other arithmetic  43 us (12%)
  starting transfers between devices  37.2 us (10%)
  matrix products  35.8 us (10%)
  local copies, waits for them, and re-layouts  34.4 us (10%)
  between operations  15.4 us (4%)
    all_to_all x1, waiting for transfers between devices, body(): up_loc = lax.all_to_all(pieces, ('dp', 'rows'), 0, 0, tiled=True)  44.8 us
    all_gather x1, waiting for transfers between devices, body(): down_loc = lax.all_gather(down_loc, 'dp', axis=1, tiled=True)  43.2 us
    reduce_scatter x1, waiting for transfers between devices, body(): lax.psum_scatter(jnp.stack([mlp_terms, norm_terms]).astype(jnp.bfloat16),...  42.1 us
    reduce_scatter x1, waiting for transfers between devices, body(): lax.psum_scatter(up_part.astype(jnp.bfloat16), 'dp', scatter_dimension=0,...  27.8 us
    all_to_all x1, waiting for transfers between devices, body(): lax.all_to_all(grad_sums, 'rows', 1, 2, tiled=True).astype(jnp.float32)  13.8 us
    reduce_sum x1, other arithmetic, body(): average = jnp.mean(flat, axis=-1, keepdims=True)  9.44 us
    convert_element_type x1, other arithmetic, body(): grad_x = (d_out.astype(jnp.float32) + back_conv).astype(jnp.bfloat16)  8.33 us
    dot_general x1, matrix products, body(): hidden = jnp.dot(gathered, up_loc, preferred_element_type=jnp.float32)  7.49 us
  transfers between devices with their start and end apart: 14, of which 7 were waited for; matrix products, arithmetic and copies ran while one was open for 20% of the time, Pallas kernels for 0%

commit v1 on v0

--- a/solution.py
+++ b/solution.py
@@ -63,7 +63,12 @@
     up_loc = lax.all_to_all(pieces, ("dp", "rows"), 0, 0, tiled=True)
     up_loc = up_loc.reshape(dp_size * row_size * block_c, sub)
     down_loc = lax.all_to_all(w_down, "rows", 0, 1, tiled=True)
-    down_loc = lax.all_gather(down_loc, "dp", axis=1, tiled=True)
+    ring = [down_loc]
+    for hop in range(3):
+        ring.append(lax.ppermute(ring[-1], "dp", [(dev, (dev + 1) % 4) for dev in range(4)]))
+    down_loc = jnp.roll(
+        jnp.concatenate(ring[::-1], axis=1), (lax.axis_index("dp") + 1) * ring[0].shape[1], axis=1
+    )
     cotan = d_out.reshape(cells, width).astype(jnp.float32)
     back = (cotan * layer_scale).astype(jnp.bfloat16)
     rimmed = padded_2(feature_maps, (("rows", 1),), 3)

time: 357 us -> 368 us (1.031); the launches traced: 350 us -> 366 us
  starting transfers between devices: 37.2 us -> 51.4 us
  local copies, waits for them, and re-layouts: 34.4 us -> 46.2 us
  waiting for transfers between devices: 184 us -> 176 us
    ppermute x0 -> x3, waiting for transfers between devices: none -> 80.8 us  [body(): lax.ppermute(ring[-1], 'dp', [(dev, (dev + 1) % 4) for dev in range(4)])]
    all_to_all x1, waiting for transfers between devices: 44.8 us -> 0.01 us  [body(): up_loc = lax.all_to_all(pieces, ('dp', 'rows'), 0, 0, tiled=True)]
    all_gather x1 -> x0, waiting for transfers between devices: 43.2 us -> none  [body(): down_loc = lax.all_gather(down_loc, 'dp', axis=1, tiled=True)]
    ppermute x0 -> x3, starting transfers between devices: none -> 14.7 us  [body(): lax.ppermute(ring[-1], 'dp', [(dev, (dev + 1) % 4) for dev in range(4)])]
    unnamed x126 -> x135, local copies, waits for them, and re-layouts: 3.69 us -> 14.9 us
  transfers between devices with their start and end apart: 14 -> 16, of which waited for: 7 -> 8; matrix products, arithmetic and copies ran while one was open for 20% -> 20% of each run, Pallas kernels for 0% -> 0%
where the time goes in v1:
time: 368 us; the launch traced here: 366 us
  waiting for transfers between devices  176 us (48%)
  starting transfers between devices  51.4 us (14%)
  local copies, waits for them, and re-layouts  46.2 us (13%)
  other arithmetic  43 us (12%)
  matrix products  34.3 us (9%)
  between operations  15.2 us (4%)
    ppermute x3, waiting for transfers between devices, body(): lax.ppermute(ring[-1], 'dp', [(dev, (dev + 1) % 4) for dev in range(4)])  80.8 us
    reduce_scatter x1, waiting for transfers between devices, body(): lax.psum_scatter(jnp.stack([mlp_terms, norm_terms]).astype(jnp.bfloat16),...  42.7 us
    reduce_scatter x1, waiting for transfers between devices, body(): lax.psum_scatter(up_part.astype(jnp.bfloat16), 'dp', scatter_dimension=0,...  27.4 us
    unnamed x135, local copies, waits for them, and re-layouts  14.9 us
    ppermute x3, starting transfers between devices, body(): lax.ppermute(ring[-1], 'dp', [(dev, (dev + 1) % 4) for dev in range(4)])  14.7 us
    all_to_all x1, waiting for transfers between devices, body(): lax.all_to_all(grad_sums, 'rows', 1, 2, tiled=True).astype(jnp.float32)  13.6 us
    reduce_sum x1, other arithmetic, body(): average = jnp.mean(flat, axis=-1, keepdims=True)  9.44 us
    convert_element_type x1, other arithmetic, body(): grad_x = (d_out.astype(jnp.float32) + back_conv).astype(jnp.bfloat16)  8.33 us
  transfers between devices with their start and end apart: 16, of which 8 were waited for; matrix products, arithmetic and copies ran while one was open for 20% of the time, Pallas kernels for 0%

profile of v1, /device:TPU:0, one launch (start us, length us, event | category | flops | bytes accessed | tf_op | source)
XLA Modules:
  0.0 366.5 jit_solution(7568020447722689715)
XLA Ops:
  19.2 9.4 %fusion.116 = (f32[4,32]{1,0:T(4,128)S(1)}, f32[1,4,32,1536]{3,2,1,0:T(8,128)S(1)}) fusion(f32[1536]{0:T(1024)S(1)} %get-tuple-element.119, f32[1536]{0:T(1024)S(1)} %get-tuple-element.120, f32[1536]{0:T(1024)S(1)} %get-tuple-element.73, f32[1536]{0:T(1024)S(1)} %get-tuple-element.74, f32[1,10,32,1536]{3,2,1,0:T(8,128)S(1)} %maximum_convert_fusion, ...), kind=kLoop, calls=%fused_computation.344 | loop fusion | flops 19267456 | bytes 8641024 | tf_op jit(solution)/shard_map/reduce_sum | solution.py:85
  31.9 6.1 %all-to-all-start.1 = ((bf16[4,768,96]{1,2,0:T(8,128)(2,1)}), bf16[4,768,96]{1,2,0:T(8,128)(2,1)S(1)}, u32[]{:S(2)}, u32[]{:S(2)}) async-start(bf16[4,768,96]{1,2,0:T(8,128)(2,1)} %bitcast.94), calls=%async_computation.1 | async-start | bytes 1179648 | tf_op jit(solution)/shard_map/all_to_all | solution.py:65
  42.5 7.0 %all-to-all-done.1 = bf16[4,768,96]{1,2,0:T(8,128)(2,1)S(1)} async-done(((bf16[4,768,96]{1,2,0:T(8,128)(2,1)}), bf16[4,768,96]{1,2,0:T(8,128)(2,1)S(1)}, u32[]{:S(2)}, u32[]{:S(2)}) %all-to-all-start.1) | async-done | bytes 589856 | tf_op jit(solution)/shard_map/all_to_all | solution.py:65
  52.2 5.3 %all-to-all-start = ((bf16[16,96,768]{2,1,0:T(8,128)(2,1)}), bf16[16,96,768]{2,1,0:T(8,128)(2,1)}, u32[]{:S(2)}, u32[]{:S(2)}) async-start(bf16[16,96,768]{2,1,0:T(8,128)(2,1)} %bitcast.84), calls=%async_computation | async-start | bytes 4718592 | tf_op jit(solution)/shard_map/all_to_all | solution.py:63
  59.5 53.9 %collective-permute-done.2 = bf16[768,384]{0,1:T(8,128)(2,1)S(1)} collective-permute-done((bf16[768,384]{0,1:T(8,128)(2,1)S(1)}, bf16[768,384]{0,1:T(8,128)(2,1)S(1)}, u32[]{:S(2)}, u32[]{:S(2)}) %collective-permute-start.2) | collective-permute-done | bytes 589856 | tf_op jit(solution)/shard_map/ppermute | solution.py:68
  114.2 10.2 %collective-permute-start.3 = (bf16[768,384]{0,1:T(8,128)(2,1)S(1)}, bf16[768,384]{0,1:T(8,128)(2,1)}, u32[]{:S(2)}, u32[]{:S(2)}) collective-permute-start(bf16[768,384]{0,1:T(8,128)(2,1)S(1)} %collective-permute-done.2), channel_id=1, source_target_pairs={{0,8},{8,16},{16,24},{24,0},{1,9},{9,17},{17,25},{25,1},{2,10},{10... | collective-permute-start | bytes 1769480 | tf_op jit(solution)/shard_map/ppermute | solution.py:68
  124.4 12.4 %collective-permute-done.3 = bf16[768,384]{0,1:T(8,128)(2,1)} collective-permute-done((bf16[768,384]{0,1:T(8,128)(2,1)S(1)}, bf16[768,384]{0,1:T(8,128)(2,1)}, u32[]{:S(2)}, u32[]{:S(2)}) %collective-permute-start.3) | collective-permute-done | bytes 589856 | tf_op jit(solution)/shard_map/ppermute | solution.py:68
  139.4 14.5 %collective-permute-done.4 = bf16[768,384]{0,1:T(8,128)(2,1)} collective-permute-done((bf16[768,384]{0,1:T(8,128)(2,1)}, bf16[768,384]{0,1:T(8,128)(2,1)}, u32[]{:S(2)}, u32[]{:S(2)}) %collective-permute-start.4) | collective-permute-done | bytes 589856 | tf_op jit(solution)/shard_map/ppermute | solution.py:68
  165.1 5.1 %multiply_convert_fusion = (bf16[1024,768]{1,0:T(8,128)(2,1)S(1)}, f32[1024,768]{1,0:T(8,128)S(1)}) fusion(bf16[1536,768]{1,0:T(8,128)(2,1)} %bitcast.5, bf16[2,1024,1536]{2,1,0:T(8,128)(2,1)} %all-gather.2.cloned.1.call-done), kind=kOutput, calls=%fused_computation.100 | convolution fusion | flops 2419851264 | bytes 10223616 | tf_op jit(solution)/shard_map/dot_general | solution.py:93
  170.2 5.2 %fusion = bf16[1,1024,1536]{2,1,0:T(8,128)(2,1)S(1)} fusion(bf16[1024,768]{1,0:T(8,128)(2,1)S(1)} %get-tuple-element.133, bf16[768,3072]{0,1:T(8,128)(2,1)} %constant_dynamic-update-slice_fusion, s32[]{:T(128)S(6)} %select_n.14), kind=kOutput, calls=%fused_computation.90 | convolution fusion | flops 2417491968 | bytes 7077892 | tf_op jit(solution)/shard_map/dot_general | solution.py:95
  175.5 5.2 %fusion.7 = bf16[1024,768]{1,0:T(8,128)(2,1)S(1)} fusion(f32[1024,768]{1,0:T(8,128)S(1)} %get-tuple-element.134, bf16[768,3072]{0,1:T(8,128)(2,1)} %constant_dynamic-update-slice_fusion, s32[]{:T(128)S(6)} %select_n.14, bf16[2,1024,1536]{2,1,0:T(8,128)(2,1)S(1)} %copy-done.60), kind=kOutput, calls=%fused_computation.97 | convolution fusion | flops 2423783424 | bytes 10223620 | tf_op jit(solution)/shard_map/dot_general | solution.py:99
  180.7 5.1 %fusion.1 = bf16[1,1024,1536]{2,1,0:T(8,128)(2,1)S(1)} fusion(bf16[1024,768]{1,0:T(8,128)(2,1)S(1)} %fusion.7, bf16[1536,768]{1,0:T(8,128)(2,1)} %bitcast.5), kind=kOutput, calls=%fused_computation.91 | convolution fusion | flops 2417491968 | bytes 7077888 | tf_op jit(solution)/shard_map/dot_general | solution.py:106
  185.9 3.2 pad_maximum_fusion
  189.1 6.5 %convolution_convert_fusion.3 = bf16[1536,768]{1,0:T(8,128)(2,1)} fusion(bf16[1024,768]{1,0:T(8,128)(2,1)} %copy-done.62, bf16[2,1024,1536]{2,1,0:T(8,128)(2,1)} %all-gather.2.cloned.1.call-done), kind=kOutput, calls=%fused_computation.89 | convolution fusion | flops 2417098752 | bytes 7077888 | tf_op jit(solution)/shard_map/dot_general | solution.py:103
  195.6 7.2 %convolution_convert_fusion.2 = bf16[1536,768]{1,0:T(8,128)(2,1)} fusion(bf16[1024,768]{1,0:T(8,128)(2,1)} %copy-done.61, bf16[2,1024,1536]{2,1,0:T(8,128)(2,1)} %all-gather.2.cloned.1.call-done), kind=kOutput, calls=%fused_computation.88 | convolution fusion | flops 2417098752 | bytes 7077888 | tf_op jit(solution)/shard_map/dot_general | solution.py:96
  202.8 4.7 %all-to-all-start.2 = ((bf16[4,384,768]{2,1,0:T(8,128)(2,1)}), bf16[4,384,768]{2,1,0:T(8,128)(2,1)}, u32[]{:S(2)}, u32[]{:S(2)}) async-start(bf16[4,384,768]{2,1,0:T(8,128)(2,1)} %bitcast.93), calls=%async_computation.4 | async-start | bytes 4718592 | tf_op jit(solution)/shard_map/all_to_all | solution.py:120
  207.5 42.7 %reduce-scatter.3.cloned.1.call-done = bf16[2,128,1536]{2,1,0:T(8,128)(2,1)} async-done(((bf16[2,1024,1536]{2,1,0:T(8,128)(2,1)}), bf16[2,128,1536]{2,1,0:T(8,128)(2,1)}) %reduce-scatter.3.cloned.1.call-update) | async-done | bytes 786448 | tf_op jit(solution)/shard_map/reduce_scatter | solution.py:109
  269.0 4.7 %all-to-all-start.3 = ((f32[32,2,1536]{2,1,0:T(2,128)}), f32[32,2,1536]{2,1,0:T(2,128)}, u32[]{:S(2)}, u32[]{:S(2)}) async-start(f32[32,2,1536]{2,1,0:T(2,128)} %reshape.563), calls=%async_computation.5 | async-start | bytes 786432 | tf_op jit(solution)/shard_map/all_to_all | solution.py:46
  279.5 27.4 %reduce-scatter.5.cloned.1.call-done = bf16[384,768]{1,0:T(8,128)(2,1)} async-done(((bf16[1536,768]{1,0:T(8,128)(2,1)}), bf16[384,768]{1,0:T(8,128)(2,1)}) %reduce-scatter.5.cloned.1.call-update) | async-done | bytes 589840 | tf_op jit(solution)/shard_map/reduce_scatter | solution.py:121
  312.0 4.9 %all-to-all-start.4 = ((f32[32,2,1536]{2,1,0:T(2,128)}), f32[32,2,1536]{2,1,0:T(2,128)S(1)}, u32[]{:S(2)}, u32[]{:S(2)}) async-start(f32[32,2,1536]{2,1,0:T(2,128)} %broadcast_in_dim.11), calls=%async_computation.6 | async-start | bytes 786432 | tf_op jit(solution)/shard_map/all_to_all | solution.py:48
  316.9 8.3 %fusion.101 = bf16[1,4,32,1536]{3,2,1,0:T(8,128)(2,1)} fusion(f32[1,10,32,1536]{3,2,1,0:T(8,128)S(1)} %maximum_convert_fusion.1, f32[1536]{0:T(1024)} %copy-done.17, f32[1536]{0:T(1024)} %copy-done.18, f32[1536]{0:T(1024)} %copy-done.20, f32[1536]{0:T(1024)} %copy-done.21, f32[1536]{0:T(1024)} %copy-done.22, f32[1536]{0:T(1024)} %copy-done.23, ...), kind=kLoop, calls=%fused_computation.197 | loop fusion | flops 19660800 | bytes 8562688 | tf_op jit(solution)/shard_map/convert_element_type | solution.py:147
  325.2 4.8 %all-to-all-done.4 = f32[32,2,1536]{2,1,0:T(2,128)S(1)} async-done(((f32[32,2,1536]{2,1,0:T(2,128)}), f32[32,2,1536]{2,1,0:T(2,128)S(1)}, u32[]{:S(2)}, u32[]{:S(2)}) %all-to-all-start.4) | async-done | bytes 393248 | tf_op jit(solution)/shard_map/all_to_all | solution.py:48
  334.0 3.8 %all-to-all-start.5 = ((bf16[2,384,768]{2,0,1:T(2,128)(2,1)}), bf16[2,384,768]{2,0,1:T(2,128)(2,1)S(1)}, u32[]{:S(2)}, u32[]{:S(2)}) async-start(bf16[2,384,768]{2,0,1:T(2,128)(2,1)} %copy.37), calls=%async_computation.7 | async-start | bytes 2359296 | tf_op jit(solution)/shard_map/all_to_all | solution.py:152
  339.8 13.6 %all-to-all-done.5 = bf16[2,384,768]{2,0,1:T(2,128)(2,1)S(1)} async-done(((bf16[2,384,768]{2,0,1:T(2,128)(2,1)}), bf16[2,384,768]{2,0,1:T(2,128)(2,1)S(1)}, u32[]{:S(2)}, u32[]{:S(2)}) %all-to-all-start.5) | async-done | bytes 1179680 | tf_op jit(solution)/shard_map/all_to_all | solution.py:152
  (252 shorter events, 80.0 us)
Async XLA Ops:
  7.2 158.0 %all-gather.2.cloned.1.call-start = ((), (), s32[]{:S(2)}) async-start(), calls=%async_computation.8 | async-start | bytes 7077888 | tf_op jit(solution)/shard_map/all_gather | solution.py:91
  8.3 9.7 %collective-permute-start = (bf16[1,3,32,1536]{3,2,1,0:T(8,128)(2,1)S(1)}, bf16[1,3,32,1536]{3,2,1,0:T(8,128)(2,1)S(1)}, u32[]{:S(2)}, u32[]{:S(2)}) collective-permute-start(bf16[1,3,32,1536]{3,2,1,0:T(8,128)(2,1)S(1)} %get-tuple-element.131), channel_id=1, source_target_pairs={{0,1},{1,2},{2,3},{4,5},{5,6},{6,7},{8,9},{9,10},{10,11},{12,13},{... | collective-permute-start | bytes 884744 | tf_op jit(solution)/shard_map/ppermute | solution.py:22
  10.7 7.3 %collective-permute-start.1 = (bf16[1,3,32,1536]{3,2,1,0:T(8,128)(2,1)S(1)}, bf16[1,3,32,1536]{3,2,1,0:T(8,128)(2,1)S(1)}, u32[]{:S(2)}, u32[]{:S(2)}) collective-permute-start(bf16[1,3,32,1536]{3,2,1,0:T(8,128)(2,1)S(1)} %get-tuple-element.132), channel_id=1, source_target_pairs={{1,0},{2,1},{3,2},{5,4},{6,5},{7,6},{9,8},{10,9},{11,10},{13,12},{... | collective-permute-start | bytes 884744 | tf_op jit(solution)/shard_map/ppermute | solution.py:23
  13.4 15.3 %copy-start.8 = (f32[1536]{0:T(1024)}, f32[1536]{0:T(1024)S(1)}, u32[]{:S(2)}) copy-start(f32[1536]{0:T(1024)S(1)} %get-tuple-element.111) | copy-start | bytes 18436
  13.4 15.3 %copy-start.10 = (f32[1536]{0:T(1024)}, f32[1536]{0:T(1024)S(1)}, u32[]{:S(2)}) copy-start(f32[1536]{0:T(1024)S(1)} %get-tuple-element.112) | copy-start | bytes 18436
  13.4 15.3 %copy-start.11 = (f32[1536]{0:T(1024)}, f32[1536]{0:T(1024)S(1)}, u32[]{:S(2)}) copy-start(f32[1536]{0:T(1024)S(1)} %get-tuple-element.113) | copy-start | bytes 18436
  13.4 15.3 %copy-start.12 = (f32[1536]{0:T(1024)}, f32[1536]{0:T(1024)S(1)}, u32[]{:S(2)}) copy-start(f32[1536]{0:T(1024)S(1)} %get-tuple-element.114) | copy-start | bytes 18436
  13.5 15.3 %copy-start.13 = (f32[1536]{0:T(1024)}, f32[1536]{0:T(1024)S(1)}, u32[]{:S(2)}) copy-start(f32[1536]{0:T(1024)S(1)} %get-tuple-element.115) | copy-start | bytes 18436
  13.5 15.3 %copy-start.14 = (f32[1536]{0:T(1024)}, f32[1536]{0:T(1024)S(1)}, u32[]{:S(2)}) copy-start(f32[1536]{0:T(1024)S(1)} %get-tuple-element.116) | copy-start | bytes 18436
  13.5 15.3 %copy-start.15 = (f32[1536]{0:T(1024)}, f32[1536]{0:T(1024)S(1)}, u32[]{:S(2)}) copy-start(f32[1536]{0:T(1024)S(1)} %get-tuple-element.117) | copy-start | bytes 18436
  31.9 17.6 %all-to-all-start.1 = ((bf16[4,768,96]{1,2,0:T(8,128)(2,1)}), bf16[4,768,96]{1,2,0:T(8,128)(2,1)S(1)}, u32[]{:S(2)}, u32[]{:S(2)}) async-start(bf16[4,768,96]{1,2,0:T(8,128)(2,1)} %bitcast.94), calls=%async_computation.1 | async-start | bytes 1179648 | tf_op jit(solution)/shard_map/all_to_all | solution.py:65
  52.2 112.9 %all-to-all-start = ((bf16[16,96,768]{2,1,0:T(8,128)(2,1)}), bf16[16,96,768]{2,1,0:T(8,128)(2,1)}, u32[]{:S(2)}, u32[]{:S(2)}) async-start(bf16[16,96,768]{2,1,0:T(8,128)(2,1)} %bitcast.84), calls=%async_computation | async-start | bytes 4718592 | tf_op jit(solution)/shard_map/all_to_all | solution.py:63
  57.5 192.7 %reduce-scatter.3.cloned.1.call-start = ((), (), s32[]{:S(2)}) async-start(), calls=%async_computation.9 | async-start | bytes 7077888 | tf_op jit(solution)/shard_map/reduce_scatter | solution.py:109
  57.5 55.9 %collective-permute-start.2 = (bf16[768,384]{0,1:T(8,128)(2,1)S(1)}, bf16[768,384]{0,1:T(8,128)(2,1)S(1)}, u32[]{:S(2)}, u32[]{:S(2)}) collective-permute-start(bf16[768,384]{0,1:T(8,128)(2,1)S(1)} %bitcast.85), channel_id=1, source_target_pairs={{0,8},{8,16},{16,24},{24,0},{1,9},{9,17},{17,25},{25,1},{2,10},{10... | collective-permute-start | bytes 1769480 | tf_op jit(solution)/shard_map/ppermute | solution.py:68
  114.2 22.6 %collective-permute-start.3 = (bf16[768,384]{0,1:T(8,128)(2,1)S(1)}, bf16[768,384]{0,1:T(8,128)(2,1)}, u32[]{:S(2)}, u32[]{:S(2)}) collective-permute-start(bf16[768,384]{0,1:T(8,128)(2,1)S(1)} %collective-permute-done.2), channel_id=1, source_target_pairs={{0,8},{8,16},{16,24},{24,0},{1,9},{9,17},{17,25},{25,1},{2,10},{10... | collective-permute-start | bytes 1769480 | tf_op jit(solution)/shard_map/ppermute | solution.py:68
  136.8 17.1 %collective-permute-start.4 = (bf16[768,384]{0,1:T(8,128)(2,1)}, bf16[768,384]{0,1:T(8,128)(2,1)}, u32[]{:S(2)}, u32[]{:S(2)}) collective-permute-start(bf16[768,384]{0,1:T(8,128)(2,1)} %collective-permute-done.3), channel_id=1, source_target_pairs={{0,8},{8,16},{16,24},{24,0},{1,9},{9,17},{17,25},{25,1},{2,10},{10... | collective-permute-start | bytes 1769480 | tf_op jit(solution)/shard_map/ppermute | solution.py:68
  139.4 18.3 %copy-start.4 = (bf16[768,384]{0,1:T(8,128)(2,1)S(1)}, bf16[768,384]{0,1:T(8,128)(2,1)}, u32[]{:S(2)}) copy-start(bf16[768,384]{0,1:T(8,128)(2,1)} %copy-done.3) | copy-start | bytes 1769476
  189.1 117.8 %reduce-scatter.5.cloned.1.call-start = ((), (), s32[]{:S(2)}) async-start(), calls=%async_computation.10 | async-start | bytes 2949120 | tf_op jit(solution)/shard_map/reduce_scatter | solution.py:121
  202.8 66.2 %all-to-all-start.2 = ((bf16[4,384,768]{2,1,0:T(8,128)(2,1)}), bf16[4,384,768]{2,1,0:T(8,128)(2,1)}, u32[]{:S(2)}, u32[]{:S(2)}) async-start(bf16[4,384,768]{2,1,0:T(8,128)(2,1)} %bitcast.93), calls=%async_computation.4 | async-start | bytes 4718592 | tf_op jit(solution)/shard_map/all_to_all | solution.py:120
  269.0 41.0 %all-to-all-start.3 = ((f32[32,2,1536]{2,1,0:T(2,128)}), f32[32,2,1536]{2,1,0:T(2,128)}, u32[]{:S(2)}, u32[]{:S(2)}) async-start(f32[32,2,1536]{2,1,0:T(2,128)} %reshape.563), calls=%async_computation.5 | async-start | bytes 786432 | tf_op jit(solution)/shard_map/all_to_all | solution.py:46
  273.8 34.3 %collective-permute-start.5 = (bf16[1,3,32,1536]{3,2,1,0:T(8,128)(2,1)S(1)}, bf16[1,3,32,1536]{3,2,1,0:T(8,128)(2,1)S(1)}, u32[]{:S(2)}, u32[]{:S(2)}) collective-permute-start(bf16[1,3,32,1536]{3,2,1,0:T(8,128)(2,1)S(1)} %get-tuple-element.129), channel_id=1, source_target_pairs={{0,1},{1,2},{2,3},{4,5},{5,6},{6,7},{8,9},{9,10},{10,11},{12,13},{... | collective-permute-start | bytes 884744 | tf_op jit(solution)/shard_map/ppermute | solution.py:22
  275.9 32.9 %collective-permute-start.6 = (bf16[1,3,32,1536]{3,2,1,0:T(8,128)(2,1)S(1)}, bf16[1,3,32,1536]{3,2,1,0:T(8,128)(2,1)}, u32[]{:S(2)}, u32[]{:S(2)}) collective-permute-start(bf16[1,3,32,1536]{3,2,1,0:T(8,128)(2,1)S(1)} %get-tuple-element.130), channel_id=1, source_target_pairs={{1,0},{2,1},{3,2},{5,4},{6,5},{7,6},{9,8},{10,9},{11,10},{13,12},{... | collective-permute-start | bytes 884744 | tf_op jit(solution)/shard_map/ppermute | solution.py:23
  312.0 18.1 %all-to-all-start.4 = ((f32[32,2,1536]{2,1,0:T(2,128)}), f32[32,2,1536]{2,1,0:T(2,128)S(1)}, u32[]{:S(2)}, u32[]{:S(2)}) async-start(f32[32,2,1536]{2,1,0:T(2,128)} %broadcast_in_dim.11), calls=%async_computation.6 | async-start | bytes 786432 | tf_op jit(solution)/shard_map/all_to_all | solution.py:48
  334.0 19.4 %all-to-all-start.5 = ((bf16[2,384,768]{2,0,1:T(2,128)(2,1)}), bf16[2,384,768]{2,0,1:T(2,128)(2,1)S(1)}, u32[]{:S(2)}, u32[]{:S(2)}) async-start(bf16[2,384,768]{2,0,1:T(2,128)(2,1)} %copy.37), calls=%async_computation.7 | async-start | bytes 2359296 | tf_op jit(solution)/shard_map/all_to_all | solution.py:152
  (55 other events, 512.2 us)
Sparse Core Ops, SparseCore 0:
  30.9 67.3 all-gather.1
  189.2 60.9 reduce-scatter.2
  252.6 54.2 reduce-scatter.4
